TPU v7x, 128 devices: a whole 4x4x4 slice. The times are simulated.
128 devices in a mesh: tm: 16 (over z_hi, y, core), tensor: 8 (over z_lo, x).
Axes of the slice: x: 4, y: 4, z: 4 (z_hi: 2, z_lo: 2; z = z_hi * 2 + z_lo), core: 2. Of those that a mesh axis runs over, the one named last changes fastest.
Arguments:
- hidden_in: bfloat16 [16, 2, 256, 5120], P('tm', None, None, 'tensor'), may hold values from -6 to 6
- noisy_queries: bfloat16 [16, 2, 256, 5120], P('tm', None, None, 'tensor'), may hold values from -28 to 28
- noisy_keys: bfloat16 [16, 2, 256, 5120], P('tm', None, None, 'tensor'), may hold values from -5 to 5
- noisy_values: bfloat16 [16, 2, 256, 5120], P('tm', None, None, 'tensor'), may hold values from -15 to 15
- clean_cache: bfloat16 [16, 2, 256, 5120], P('tm', None, None, 'tensor'), may hold values from -9 to 9
- out_proj: bfloat16 [5120, 5120], P('tensor'), may hold values from -0.078125 to 0.078125
- branch_in: bfloat16 [5120, 2560], P(None, 'tensor'), may hold values from -0.078125 to 0.078125
- branch_out: bfloat16 [2560, 5120], P('tensor'), may hold values from -0.125 to 0.125
- action_table: bfloat16 [128, 2560], P(None, 'tensor'), may hold values from -6 to 6
- actions: int32 [16, 4], P('tm'), may hold values from 0 to 127
- offsets: int32 [16], P('tm'), may hold values from 0 to 2, as said below
- out_grad: bfloat16 [16, 2, 256, 5120], P('tm', None, None, 'tensor'), may hold values from -6 to 6
Outputs:
- layer_out: bfloat16 [16, 2, 256, 5120], P('tm', None, None, 'tensor')
- input_grad: bfloat16 [16, 2, 256, 5120], P('tm', None, None, 'tensor')
- query_grad: bfloat16 [16, 2, 256, 5120], P('tm', None, None, 'tensor')
- key_grad: bfloat16 [16, 2, 256, 5120], P('tm', None, None, 'tensor')
- value_grad: bfloat16 [16, 2, 256, 5120], P('tm', None, None, 'tensor')
- cache_grad: float32 [16, 2, 256, 5120], P('tm', None, None, 'tensor')
- proj_weight_grad: float32 [5120, 5120], P('tensor', 'tm')
- branch_in_grad: float32 [5120, 2560], P('tm', 'tensor')
- branch_out_grad: float32 [2560, 5120], P('tensor', 'tm')
- table_grad: float32 [128, 2560], P('tm', 'tensor')
Inputs may be any that keep to these rules, and one draw needn't show every extreme that they name: offsets[c] <= c; spans 1, 2, 7, 8, 9 and the last reach min(c, 2).
All inputs are finite; a program needn't handle non-finite values.
Results may differ from a plain program's by a relative error of at most 0.013.
Values may be sent and summed in bfloat16 or wider, within the bound.
No kernel may reach another device: no remote copies, remote signals or barrier semaphores. Data moves between devices by JAX's collectives and lax.ppermute only.
A program may use at most 192 MiB of HBM per device.

v0:
```python
import jax
import jax.numpy as jnp
from jax import lax
from jax.sharding import PartitionSpec as P

HD = 128
GELU_C = 0.7978845608028654
GELU_A = 0.044715


def from_behind(value, axis, steps):
    count = lax.axis_size(axis)
    first, last = (max(0, -steps), min(count, count - steps))
    return lax.ppermute(value, axis, [(source, source + steps) for source in range(first, last)])


def gelu_value(inputs):
    inner = GELU_C * (inputs + GELU_A * inputs * inputs * inputs)
    return 0.5 * inputs * (1.0 + jnp.tanh(inner))


def gelu_slope(inputs):
    tangent = jnp.tanh(GELU_C * (inputs + GELU_A * inputs * inputs * inputs))
    return 0.5 * (1.0 + tangent) + 0.5 * inputs * (1.0 - tangent * tangent) * GELU_C * (
        1.0 + 3.0 * GELU_A * inputs * inputs
    )


def contract_rows(left, right):
    return lax.dot_general(
        left, right, (((0,), (0,)), ((), ())), preferred_element_type=jnp.float32
    )


def contract_cols(left, right):
    return lax.dot_general(
        left, right, (((1,), (1,)), ((), ())), preferred_element_type=jnp.float32
    )


def body(
    hidden_in,
    noisy_queries,
    noisy_keys,
    noisy_values,
    clean_cache,
    out_proj,
    branch_in,
    branch_out,
    action_table,
    actions,
    offsets,
    out_grad,
):
    steps_here = noisy_queries.shape[1]
    tokens_here = noisy_queries.shape[2]
    head_width = noisy_queries.shape[3]
    heads_here = head_width // HD
    model_width = out_proj.shape[1]
    row_count = steps_here * tokens_here
    action_count = actions.shape[1]
    score_scale = HD ** (-0.5)
    full_both = lax.all_gather(
        jnp.concatenate([hidden_in, out_grad], axis=0), "tensor", axis=3, tiled=True
    )
    input_rows = full_both[0].reshape(row_count, model_width)
    grad_rows = full_both[1].reshape(row_count, model_width)
    own_cache = clean_cache[0]
    nearer = from_behind(own_cache, "tm", 1)
    farther = from_behind(own_cache, "tm", 2)
    reach = offsets[0]
    allowed = jnp.concatenate(
        [
            jnp.full((tokens_here,), reach >= 2),
            jnp.full((tokens_here,), reach >= 1),
            jnp.ones((tokens_here,), bool),
        ]
    )
    block_shape = (steps_here, tokens_here, head_width)
    key_block = jnp.concatenate(
        [
            jnp.broadcast_to(farther[0], block_shape),
            jnp.broadcast_to(nearer[0], block_shape),
            noisy_keys[0],
        ],
        axis=1,
    )
    value_block = jnp.concatenate(
        [
            jnp.broadcast_to(farther[1], block_shape),
            jnp.broadcast_to(nearer[1], block_shape),
            noisy_values[0],
        ],
        axis=1,
    )
    query_heads = noisy_queries[0].reshape(steps_here, tokens_here, heads_here, HD)
    key_heads = key_block.reshape(steps_here, 3 * tokens_here, heads_here, HD)
    value_heads = value_block.reshape(steps_here, 3 * tokens_here, heads_here, HD)
    scores = (
        jnp.einsum("sqhe,skhe->shqk", query_heads, key_heads, preferred_element_type=jnp.float32)
        * score_scale
    )
    masked = jnp.where(allowed[None, None, None, :], scores, -1e30)
    largest = jnp.max(masked, axis=-1, keepdims=True)
    raised = jnp.exp(masked - largest)
    probs = raised / jnp.sum(raised, axis=-1, keepdims=True)
    probs_low = probs.astype(jnp.bfloat16)
    attended = (
        jnp.einsum("shqk,skhe->sqhe", probs_low, value_heads, preferred_element_type=jnp.float32)
        .astype(jnp.bfloat16)
        .reshape(row_count, head_width)
    )
    onehot = (actions[0][:, None] == jnp.arange(action_table.shape[0])[None, :]).astype(
        jnp.bfloat16
    )
    action_rows = jnp.dot(onehot, action_table, preferred_element_type=jnp.float32)
    branch_width = branch_in.shape[1]
    pre_act = (
        jnp.dot(input_rows, branch_in, preferred_element_type=jnp.float32).reshape(
            steps_here, action_count, tokens_here // action_count, branch_width
        )
        + action_rows[None, :, None, :]
    )
    pre_act = pre_act.reshape(row_count, branch_width)
    branch_act = gelu_value(pre_act).astype(jnp.bfloat16)
    partial_value = jnp.dot(attended, out_proj, preferred_element_type=jnp.float32) + jnp.dot(
        branch_act, branch_out, preferred_element_type=jnp.float32
    )
    layer_sum = lax.psum_scatter(
        partial_value.reshape(1, steps_here, tokens_here, model_width).astype(jnp.bfloat16),
        "tensor",
        scatter_dimension=3,
        tiled=True,
    ).astype(jnp.float32)
    layer_out = (hidden_in.astype(jnp.float32) + layer_sum).astype(jnp.bfloat16)
    attended_grad = contract_cols(grad_rows, out_proj).astype(jnp.bfloat16)
    pre_grad = (contract_cols(grad_rows, branch_out) * gelu_slope(pre_act)).astype(jnp.bfloat16)
    tm_count = lax.axis_size("tm")
    col_block = model_width // tm_count
    grad_split = grad_rows.reshape(row_count, tm_count, col_block)
    in_term = jnp.einsum(
        "rjk,rn->jkn",
        input_rows.reshape(row_count, tm_count, model_width // tm_count),
        pre_grad,
        preferred_element_type=jnp.float32,
    )
    out_term = jnp.einsum("rk,rjn->jkn", branch_act, grad_split, preferred_element_type=jnp.float32)
    grouped = jnp.sum(
        pre_grad.reshape(
            steps_here, action_count, tokens_here // action_count, branch_width
        ).astype(jnp.float32),
        axis=(0, 2),
    )
    table_term = jnp.dot(onehot.astype(jnp.float32).T, grouped, precision=lax.Precision.HIGHEST)
    proj_term = jnp.einsum("rk,rjn->jkn", attended, grad_split, preferred_element_type=jnp.float32)
    table_rows = table_term.shape[0] // tm_count
    pieces = (
        proj_term.astype(jnp.bfloat16),
        in_term.astype(jnp.bfloat16),
        out_term.astype(jnp.bfloat16),
        table_term.reshape(tm_count, table_rows, branch_width).astype(jnp.bfloat16),
    )
    merged = lax.psum_scatter(
        jnp.concatenate(pieces, axis=1), "tm", scatter_dimension=0, tiled=True
    )[0].astype(jnp.float32)
    bounds = [0]
    for piece in pieces:
        bounds.append(bounds[-1] + piece.shape[1])
    summed = tuple((merged[bounds[i] : bounds[i + 1]] for i in range(4)))
    input_term = contract_cols(pre_grad, branch_in)
    input_sum = lax.psum_scatter(
        input_term.reshape(1, steps_here, tokens_here, model_width).astype(jnp.bfloat16),
        "tensor",
        scatter_dimension=3,
        tiled=True,
    ).astype(jnp.float32)
    input_grad = (out_grad.astype(jnp.float32) + input_sum).astype(jnp.bfloat16)
    weight_grads = (summed, input_grad)
    grad_heads = attended_grad.reshape(steps_here, tokens_here, heads_here, HD)
    value_all = jnp.einsum(
        "shqk,sqhe->skhe", probs_low, grad_heads, preferred_element_type=jnp.float32
    )
    prob_grad = jnp.einsum(
        "sqhe,skhe->shqk", grad_heads, value_heads, preferred_element_type=jnp.float32
    )
    centre = jnp.sum(prob_grad * probs, axis=-1, keepdims=True)
    score_grad = (probs * (prob_grad - centre) * score_scale).astype(jnp.bfloat16)
    query_grad = (
        jnp.einsum("shqk,skhe->sqhe", score_grad, key_heads, preferred_element_type=jnp.float32)
        .astype(jnp.bfloat16)
        .reshape(1, steps_here, tokens_here, head_width)
    )
    key_all = jnp.einsum(
        "shqk,sqhe->skhe", score_grad, query_heads, preferred_element_type=jnp.float32
    ).reshape(steps_here, 3 * tokens_here, head_width)
    value_all = value_all.reshape(steps_here, 3 * tokens_here, head_width)
    own_key = key_all[:, 2 * tokens_here :].astype(jnp.bfloat16)[None]
    own_value = value_all[:, 2 * tokens_here :].astype(jnp.bfloat16)[None]
    toward_far = jnp.stack(
        [jnp.sum(key_all[:, :tokens_here], axis=0), jnp.sum(value_all[:, :tokens_here], axis=0)]
    )
    toward_near = jnp.stack(
        [
            jnp.sum(key_all[:, tokens_here : 2 * tokens_here], axis=0),
            jnp.sum(value_all[:, tokens_here : 2 * tokens_here], axis=0),
        ]
    )
    from_next = from_behind(toward_near.astype(jnp.bfloat16), "tm", -1).astype(toward_near.dtype)
    from_after = from_behind(toward_far.astype(jnp.bfloat16), "tm", -2).astype(toward_far.dtype)
    received = from_next + from_after
    attention_grads = (query_grad, own_key, own_value, received[None])
    summed, input_grad = weight_grads
    query_grad, own_key, own_value, cache_grad = attention_grads
    return (
        layer_out,
        input_grad,
        query_grad,
        own_key,
        own_value,
        cache_grad,
        summed[0],
        summed[1],
        summed[2],
        summed[3],
    )


def solution(mesh):
    in_specs = (
        P("tm", None, None, "tensor"),
        P("tm", None, None, "tensor"),
        P("tm", None, None, "tensor"),
        P("tm", None, None, "tensor"),
        P("tm", None, None, "tensor"),
        P("tensor", None),
        P(None, "tensor"),
        P("tensor", None),
        P(None, "tensor"),
        P("tm", None),
        P("tm"),
        P("tm", None, None, "tensor"),
    )
    out_specs = (
        P("tm", None, None, "tensor"),
        P("tm", None, None, "tensor"),
        P("tm", None, None, "tensor"),
        P("tm", None, None, "tensor"),
        P("tm", None, None, "tensor"),
        P("tm", None, None, "tensor"),
        P("tensor", "tm"),
        P("tm", "tensor"),
        P("tensor", "tm"),
        P("tm", "tensor"),
    )
    return jax.shard_map(body, mesh=mesh, in_specs=in_specs, out_specs=out_specs, check_vma=False)
```

profile of v0, /device:TPU:0, one launch (start us, length us, event | category | flops | bytes accessed | tf_op | source)
XLA Modules:
  0.0 501.3 jit_solution(12382191441929231244)
XLA Ops:
  7.2 2.6 pad_maximum_fusion.10
  11.0 113.4 %all-gather.2.cloned.1.call-done = bf16[2,2,256,5120]{3,2,1,0:T(8,128)(2,1)} async-done(((bf16[2,2,256,640]{3,2,1,0:T(8,128)(2,1)}), bf16[2,2,256,5120]{3,2,1,0:T(8,128)(2,1)}) %all-gather.2.cloned.1.call-update) | async-done | bytes 10485776 | tf_op jit(solution)/shard_map/all_gather | solution.py:63
  124.4 8.7 %fusion.81 = (bf16[1,2,256,5120]{3,2,1,0:T(8,128)(2,1)}, bf16[1,2,256,5120]{3,2,1,0:T(8,128)(2,1)}) fusion(bf16[2,2,256,5120]{3,2,1,0:T(8,128)(2,1)} %all-gather.2.cloned.1.call-done), kind=kLoop, calls=%fused_computation.105 | loop fusion | bytes 20971520 | tf_op jit(solution)/shard_map/slice | solution.py:67
  133.1 6.5 %fusion.49 = (bf16[2,4,64,320]{3,2,1,0:T(8,128)(2,1)}, f32[2,4,64,320]{3,2,1,0:T(8,128)}) fusion(f32[4,320]{1,0:T(4,128)S(1)} %fusion.65, bf16[2,4,64,5120]{3,2,1,0:T(8,128)(2,1)} %bitcast.132, bf16[5120,320]{0,1:T(8,128)(2,1)S(1)} %copy-done), kind=kOutput, calls=%fused_computation.58 | convolution fusion | flops 1679360000 | bytes 9507840 | tf_op jit(solution)/shard_map/dot_general | solution.py:119
  139.6 2.2 copy.145
  141.8 5.7 %fusion.44 = bf16[512,320]{0,1:T(8,128)(2,1)S(1)} fusion(bf16[512,5120]{1,0:T(8,128)(2,1)} %bitcast.130, bf16[320,5120]{1,0:T(8,128)(2,1)} %param.19, f32[512,320]{0,1:T(8,128)} %copy.145), kind=kOutput, calls=%fused_computation.48 | convolution fusion | flops 1680834560 | bytes 9502720 | tf_op jit(solution)/shard_map/dot_general | solution.py:36
  148.3 4.7 convolution_convert_fusion
  153.0 13.6 %copy.192 = bf16[1,2,256,5120]{2,1,0,3:T(2,128)(2,1)} copy(bf16[1,2,256,5120]{3,2,1,0:T(8,128)(2,1)} %bitcast.137) | data formatting | bytes 10485760
  166.6 5.7 %copy.200 = bf16[640,8,2,256]{3,1,2,0:T(8,128)(2,1)} copy(bf16[640,8,2,256]{3,2,1,0:T(2,128)(2,1)} %bitcast.135) | data formatting | bytes 10485760
  174.5 2.4 collective-permute-start.1
  176.9 4.2 collective-permute-start
  184.0 1.8 fusion.83
  186.1 9.1 %collective-permute-done = bf16[2,256,640]{1,2,0:T(8,128)(2,1)} collective-permute-done((bf16[2,256,640]{1,2,0:T(8,128)(2,1)}, bf16[2,256,640]{1,2,0:T(8,128)(2,1)}, u32[]{:S(2)}, u32[]{:S(2)}) %collective-permute-start) | collective-permute-done | bytes 655392 | tf_op jit(solution)/shard_map/ppermute | solution.py:14
  195.2 1.8 fusion.82
  200.6 2.6 fusion.84
  204.6 2.6 copy-done.27
  209.5 4.4 fusion.85
  213.9 4.9 add_convert_fusion
  218.8 13.6 %copy.190 = bf16[1,2,256,5120]{2,1,0,3:T(2,128)(2,1)} copy(bf16[1,2,256,5120]{3,2,1,0:T(8,128)(2,1)} %bitcast.129) | data formatting | bytes 10485760
  232.4 5.7 %copy.199 = bf16[640,8,2,256]{3,1,2,0:T(8,128)(2,1)} copy(bf16[640,8,2,256]{3,2,1,0:T(2,128)(2,1)} %bitcast.136) | data formatting | bytes 10485760
  238.2 11.3 %reshape.134 = bf16[512,16,320]{2,1,0:T(8,128)(2,1)} reshape(bf16[1,2,256,5120]{3,2,1,0:T(8,128)(2,1)} %get-tuple-element.54) | data formatting | bytes 10485760 | tf_op jit(solution)/shard_map/reshape;reshape;squeeze | solution.py:140
  249.5 11.0 %reshape.135 = bf16[512,16,320]{2,1,0:T(8,128)(2,1)} reshape(bf16[1,2,256,5120]{3,2,1,0:T(8,128)(2,1)} %get-tuple-element.55) | data formatting | bytes 10485760 | tf_op jit(solution)/shard_map/reshape;reshape;squeeze | solution.py:143
  260.7 8.6 %copy.186 = bf16[512,16,320]{0,2,1:T(8,128)(2,1)} copy(bf16[512,16,320]{2,1,0:T(8,128)(2,1)} %reshape.134) | data formatting | bytes 10485760 | tf_op jit(solution)/shard_map/reshape;reshape;squeeze | solution.py:140
  270.4 7.9 %convert_bitcast_fusion = bf16[16,320,320]{1,2,0:T(8,128)(2,1)} fusion(bf16[512,16,320]{0,2,1:T(8,128)(2,1)} %copy.186, bf16[512,320,1]{1,0,2:T(8,128)(2,1)} %bitcast.171), kind=kOutput, calls=%fused_computation.16 | convolution fusion | flops 1679360000 | bytes 8847360 | tf_op jit(solution)/shard_map/rk,rjn->jkn/dot_general | solution.py:147
  278.3 7.5 %fusion.23 = bf16[16,320,320]{1,2,0:T(8,128)(2,1)} fusion(bf16[512,16,320]{2,1,0:T(8,128)(2,1)} %reshape.135, bf16[512,320]{0,1:T(8,128)(2,1)S(1)} %copy-done.18), kind=kOutput, calls=%fused_computation.25 | convolution fusion | flops 1679360000 | bytes 8847360 | tf_op jit(solution)/shard_map/rjk,rn->jkn/dot_general | solution.py:141
  285.8 6.3 %fusion.9 = bf16[16,640,320]{1,2,0:T(8,128)(2,1)} fusion(bf16[512,16,320]{0,2,1:T(8,128)(2,1)S(1)} %bitcast.141, bf16[512,640]{0,1:T(8,128)(2,1)S(1)} %bitcast.152), kind=kOutput, calls=%fused_computation.15 | convolution fusion | flops 3358720000 | bytes 12451840 | tf_op jit(solution)/shard_map/rk,rjn->jkn/dot_general | solution.py:155
  292.1 22.7 %concatenate.27 = bf16[16,1288,320]{1,2,0:T(8,128)(2,1)} concatenate(bf16[16,640,320]{1,2,0:T(8,128)(2,1)} %fusion.9, bf16[16,320,320]{1,2,0:T(8,128)(2,1)} %fusion.23, bf16[16,320,320]{1,2,0:T(8,128)(2,1)} %convert_bitcast_fusion, bf16[16,8,320]{1,2,0:T(8,128)(2,1)S(1)} %copy.169), dimensions={1} | concatenate | bytes 26378240 | tf_op jit(solution)/shard_map/concatenate | solution.py:164
  314.9 9.6 %convolution_convert_fusion.2 = bf16[512,640]{1,0:T(8,128)(2,1)} fusion(bf16[512,5120]{1,0:T(8,128)(2,1)} %bitcast.131, bf16[640,5120]{1,0:T(8,128)(2,1)} %param.17), kind=kOutput, calls=%fused_computation.36 | convolution fusion | flops 3355770880 | bytes 12451840 | tf_op jit(solution)/shard_map/dot_general | solution.py:36
  324.5 1.8 reshape.140
  327.6 5.0 fusion.26
  332.6 1.9 copy-done.4
  335.6 4.4 fusion.31
  340.1 14.9 %fusion.13 = f32[2,5,768,128]{2,3,1,0:T(8,128)} fusion(bf16[2,256,5,128]{1,3,2,0:T(8,128)(2,1)S(1)} %bitcast.148, f32[2,5,256,768]{2,3,1,0:T(8,128)} %fusion.31, f32[2,5,256,768]{2,3,1,0:T(8,128)} %copy-done.27, f32[2,5,256]{2,1,0:T(8,128)S(1)} %get-tuple-element.62), kind=kOutput, calls=%fused_computation.17 | convolution fusion | flops 517082368 | bytes 20326400 | tf_op jit(solution)/shard_map/shqk,sqhe->skhe/dot_general | solution.py:193
  355.0 2.5 slice_reduce_fusion.3
  361.9 1.6 slice.88
  363.5 1.6 slice.89
  365.1 14.1 %fusion.35 = bf16[2,5,128,256]{3,2,1,0:T(8,128)(2,1)} fusion(f32[2,5,256,768]{2,3,1,0:T(8,128)} %fusion.31, bf16[2,256,5,128]{3,1,2,0:T(8,128)(2,1)S(1)} %copy.140, bf16[2,256,5,128]{3,1,2,0:T(8,128)(2,1)S(1)} %copy-done.9, bf16[2,256,5,128]{3,1,2,0:T(8,128)(2,1)S(1)} %copy-done.11, f32[2,5,256,768]{2,3,1,0:T(8,128)} %copy-done.27, ...), kind=kOutput, calls=%fused_computation.35 | convolution fusion | flops 523308288 | bytes 18360320 | tf_op jit(solution)/shard_map/shqk,skhe->sqhe/dot_general | solution.py:189
  379.2 2.2 copy.170
  383.5 1.4 add_bitcast_fusion
  384.9 1.5 copy.171
  386.4 2.0 reshape.139
  388.5 1.9 copy.193
  390.4 2.0 reshape.137
  392.4 1.9 copy.191
  394.4 3.2 add_convert_fusion.1
  397.6 88.6 %reduce-scatter.8.cloned.1.call-done = bf16[1,1288,320]{1,2,0:T(8,128)(2,1)} async-done(((bf16[16,1288,320]{1,2,0:T(8,128)(2,1)}), bf16[1,1288,320]{1,2,0:T(8,128)(2,1)}) %reduce-scatter.8.cloned.1.call-update) | async-done | bytes 824336 | tf_op jit(solution)/shard_map/reduce_scatter | solution.py:163
  489.5 2.0 copy.172
  491.5 2.0 copy.173
  (115 shorter events, 27.7 us)
Async XLA Ops:
  7.2 125.9 %copy-start = (bf16[5120,320]{0,1:T(8,128)(2,1)S(1)}, bf16[5120,320]{0,1:T(8,128)(2,1)}, u32[]{:S(2)}) copy-start(bf16[5120,320]{0,1:T(8,128)(2,1)} %param.18) | copy-start | bytes 9830404
  7.2 117.2 %all-gather.2.cloned.1.call-start = ((), (), s32[]{:S(2)}) async-start(), calls=%async_computation.3 | async-start | bytes 11796480 | tf_op jit(solution)/shard_map/all_gather | solution.py:63
  9.9 376.5 %reduce-scatter.12.cloned.1.call-start = ((), (), s32[]{:S(2)}) async-start(), calls=%async_computation.6 | async-start | bytes 5898240
  147.6 0.7 copy-start.16
  172.3 1.1 copy-start.23
  172.3 8.8 %copy-start.24 = (bf16[1,2,256,640]{3,2,1,0:T(8,128)(2,1)S(1)}, bf16[1,2,256,640]{3,2,1,0:T(8,128)(2,1)}, u32[]{:S(2)}) copy-start(bf16[1,2,256,640]{3,2,1,0:T(8,128)(2,1)} %param.15) | copy-start | bytes 1966084
  172.3 9.1 %copy-start.25 = (bf16[1,2,256,640]{3,2,1,0:T(8,128)(2,1)S(1)}, bf16[1,2,256,640]{3,2,1,0:T(8,128)(2,1)}, u32[]{:S(2)}) copy-start(bf16[1,2,256,640]{3,2,1,0:T(8,128)(2,1)} %param.13) | copy-start | bytes 1966084
  172.3 218.1 %reduce-scatter.10.cloned.1.call-start = ((), (), s32[]{:S(2)}) async-start(), calls=%async_computation.5 | async-start | bytes 5898240
  174.5 9.6 %collective-permute-start.1 = (bf16[2,256,640]{1,2,0:T(8,128)(2,1)}, bf16[2,256,640]{1,2,0:T(8,128)(2,1)}, u32[]{:S(2)}, u32[]{:S(2)}) collective-permute-start(bf16[2,256,640]{1,2,0:T(8,128)(2,1)} %bitcast), channel_id=1, source_target_pairs={{0,8},{8,16},{16,24},{24,32},{32,40},{40,48},{48,56},{56,64},{64,7... | collective-permute-start | bytes 1966088 | tf_op jit(solution)/shard_map/ppermute | solution.py:14
  176.9 18.3 %collective-permute-start = (bf16[2,256,640]{1,2,0:T(8,128)(2,1)}, bf16[2,256,640]{1,2,0:T(8,128)(2,1)}, u32[]{:S(2)}, u32[]{:S(2)}) collective-permute-start(bf16[2,256,640]{1,2,0:T(8,128)(2,1)} %bitcast), channel_id=1, source_target_pairs={{0,16},{8,24},{16,32},{24,40},{32,48},{40,56},{48,64},{56,72},{64,... | collective-permute-start | bytes 1966088 | tf_op jit(solution)/shard_map/ppermute | solution.py:14
  198.0 2.5 copy-start.8
  199.4 1.2 copy-start.10
  200.6 2.7 copy-start.21
  200.6 2.7 copy-start.22
  203.2 3.9 copy-start.27
  203.3 4.2 copy-start.12
  203.4 4.4 copy-start.14
  203.4 5.3 %slice-start = ((s8[6553600]{0:T(1024)(128)(4,1)}), s8[4194304]{0:T(1024)(128)(4,1)S(1)}, s32[]{:S(2)}) async-start(s8[6553600]{0:T(1024)(128)(4,1)} %bitcast.138), calls=%async_computation.7 | async-start | bytes 8388608
  203.4 6.0 %slice-start.1 = ((s8[6553600]{0:T(1024)(128)(4,1)}), s8[2359296]{0:T(1024)(128)(4,1)S(1)}, s32[]{:S(2)}) async-start(s8[6553600]{0:T(1024)(128)(4,1)} %bitcast.138), calls=%async_computation.8 | async-start | bytes 4718592
  208.6 5.3 %copy-start.5 = (bf16[80,8,2,256]{3,1,2,0:T(8,128)(2,1)}, bf16[80,8,2,256]{3,1,2,0:T(8,128)(2,1)S(1)}, u32[]{:S(2)}) copy-start(bf16[80,8,2,256]{3,1,2,0:T(8,128)(2,1)S(1)} %copy.198) | copy-start | bytes 1966084
  209.5 4.4 copy-start.2
  209.5 4.4 copy-start.3
  238.2 248.0 %reduce-scatter.8.cloned.1.call-start = ((), (), s32[]{:S(2)}) async-start(), calls=%async_computation.4 | async-start | bytes 15319040 | tf_op jit(solution)/shard_map/reduce_scatter | solution.py:163
  249.5 11.0 %copy-start.17 = (bf16[512,320]{0,1:T(8,128)(2,1)S(1)}, bf16[512,320]{0,1:T(8,128)(2,1)}, u32[]{:S(2)}) copy-start(bf16[512,320]{0,1:T(8,128)(2,1)} %copy-done.16) | copy-start | bytes 983044
  260.7 8.7 %copy-start.26 = (s32[1,4]{1,0:T(1,128)S(1)}, s32[1,4]{1,0:T(1,128)}, u32[]{:S(2)}) copy-start(s32[1,4]{1,0:T(1,128)} %param.21) | copy-start | bytes 52
  270.3 7.9 %copy-start.18 = (bf16[512,320]{0,1:T(8,128)(2,1)S(1)}, bf16[512,320]{0,1:T(8,128)(2,1)}, u32[]{:S(2)}) copy-start(bf16[512,320]{0,1:T(8,128)(2,1)} %copy-done.16) | copy-start | bytes 983044
  270.4 15.5 %slice-start.2 = ((s8[5242880]{0:T(1024)(128)(4,1)}), s8[4194304]{0:T(1024)(128)(4,1)S(1)}, s32[]{:S(2)}) async-start(s8[5242880]{0:T(1024)(128)(4,1)} %bitcast.140), calls=%async_computation.9 | async-start | bytes 8388608
  278.3 7.5 %slice-start.3 = ((s8[5242880]{0:T(1024)(128)(4,1)}), s8[1048576]{0:T(1024)(128)(4,1)S(1)}, s32[]{:S(2)}) async-start(s8[5242880]{0:T(1024)(128)(4,1)} %bitcast.140), calls=%async_computation.10 | async-start | bytes 2097152
  278.3 7.5 %copy-start.6 = (bf16[80,8,2,256]{3,1,2,0:T(8,128)(2,1)S(1)}, bf16[80,8,2,256]{3,1,2,0:T(8,128)(2,1)}, u32[]{:S(2)}) copy-start(bf16[80,8,2,256]{3,1,2,0:T(8,128)(2,1)} %copy-done.5) | copy-start | bytes 1966084
  327.6 8.0 %copy-start.7 = (bf16[2,256,5,128]{1,3,2,0:T(8,128)(2,1)S(1)}, bf16[2,256,5,128]{1,3,2,0:T(8,128)(2,1)}, u32[]{:S(2)}) copy-start(bf16[2,256,5,128]{1,3,2,0:T(8,128)(2,1)} %copy.161) | copy-start | bytes 1966084
  327.6 8.0 %copy-start.13 = (bf16[2,256,5,128]{1,3,2,0:T(8,128)(2,1)S(1)}, bf16[2,256,5,128]{1,3,2,0:T(8,128)(2,1)}, u32[]{:S(2)}) copy-start(bf16[2,256,5,128]{1,3,2,0:T(8,128)(2,1)} %copy-done.12) | copy-start | bytes 1966084
  327.6 8.0 %copy-start.15 = (bf16[2,256,5,128]{1,3,2,0:T(8,128)(2,1)S(1)}, bf16[2,256,5,128]{1,3,2,0:T(8,128)(2,1)}, u32[]{:S(2)}) copy-start(bf16[2,256,5,128]{1,3,2,0:T(8,128)(2,1)} %copy-done.14) | copy-start | bytes 1966084
  332.6 1.9 copy-start.4
  340.1 17.4 %copy-start.20 = (bf16[256,640]{0,1:T(8,128)(2,1)S(1)}, bf16[256,640]{0,1:T(8,128)(2,1)}, u32[]{:S(2)}) copy-start(bf16[256,640]{0,1:T(8,128)(2,1)} %get-tuple-element.53) | copy-start | bytes 983044
  340.1 19.6 %copy-start.19 = (bf16[256,640]{0,1:T(8,128)(2,1)S(1)}, bf16[256,640]{0,1:T(8,128)(2,1)}, u32[]{:S(2)}) copy-start(bf16[256,640]{0,1:T(8,128)(2,1)} %get-tuple-element.52) | copy-start | bytes 983044
  355.0 10.1 %copy-start.9 = (bf16[2,256,5,128]{3,1,2,0:T(8,128)(2,1)S(1)}, bf16[2,256,5,128]{3,1,2,0:T(8,128)(2,1)}, u32[]{:S(2)}) copy-start(bf16[2,256,5,128]{3,1,2,0:T(8,128)(2,1)} %copy-done.8) | copy-start | bytes 1966084
  355.0 10.1 %copy-start.11 = (bf16[2,256,5,128]{3,1,2,0:T(8,128)(2,1)S(1)}, bf16[2,256,5,128]{3,1,2,0:T(8,128)(2,1)}, u32[]{:S(2)}) copy-start(bf16[2,256,5,128]{3,1,2,0:T(8,128)(2,1)} %copy-done.10) | copy-start | bytes 1966084
  358.4 25.1 %collective-permute-start.3 = (bf16[2,256,640]{1,2,0:T(8,128)(2,1)}, bf16[2,256,640]{1,2,0:T(8,128)(2,1)}, u32[]{:S(2)}, u32[]{:S(2)}) collective-permute-start(bf16[2,256,640]{1,2,0:T(8,128)(2,1)} %pad_maximum_fusion.14), channel_id=1, source_target_pairs={{16,0},{24,8},{32,16},{40,24},{48,32},{56,40},{64,48},{72,56},{80,... | collective-permute-start | bytes 1966088 | tf_op jit(solution)/shard_map/ppermute | solution.py:14
  360.6 22.9 %collective-permute-start.2 = (bf16[2,256,640]{1,2,0:T(8,128)(2,1)}, bf16[2,256,640]{1,2,0:T(8,128)(2,1)}, u32[]{:S(2)}, u32[]{:S(2)}) collective-permute-start(bf16[2,256,640]{1,2,0:T(8,128)(2,1)} %pad_maximum_fusion.13), channel_id=1, source_target_pairs={{8,0},{16,8},{24,16},{32,24},{40,32},{48,40},{56,48},{64,56},{72,6... | collective-permute-start | bytes 1966088 | tf_op jit(solution)/shard_map/ppermute | solution.py:14
  394.4 99.9 %copy-start.1 = (bf16[5120,320]{0,1:T(8,128)(2,1)S(1)}, bf16[5120,320]{0,1:T(8,128)(2,1)}, u32[]{:S(2)}) copy-start(bf16[5120,320]{0,1:T(8,128)(2,1)} %param.18) | copy-start | bytes 9830404
Sparse Core Ops, SparseCore 0:
  10.2 114.0 all-gather.1
  172.4 81.6 reduce-scatter.11
  256.5 70.4 reduce-scatter.9
  331.4 154.7 reduce-scatter.7
where the time goes:
time: 511 us; the launch traced here: 501 us
  waiting for transfers between devices  211 us (41%)
  local copies, waits for them, and re-layouts  149 us (29%)
  matrix products  99.7 us (20%)
  other arithmetic  16.6 us (3%)
  between operations  15.5 us (3%)
  starting transfers between devices  9.37 us (2%)
    all_gather x1, waiting for transfers between devices, body(): lax.all_gather(jnp.concatenate([hidden_in, out_grad], axis=0), 'tensor',...  113 us
    reduce_scatter x1, waiting for transfers between devices, body(): lax.psum_scatter(jnp.concatenate(pieces, axis=1), 'tm', scatter_dimension...  88.6 us
    unnamed x84, local copies, waits for them, and re-layouts  68 us
    concatenate x1, local copies, waits for them, and re-layouts, body(): jnp.concatenate(pieces, axis=1)  22.7 us
    dot_general x3, matrix products, contract_cols(): lax.dot_general(left, right, (((1,), (1,)), ((), ())), preferred_element_...  20.1 us
    another operation x2, local copies, waits for them, and re-layouts, body(): grad_split = grad_rows.reshape(row_count, tm_count, col_block)  19.9 us
    dot_general x1, matrix products, body(): jnp.einsum('shqk,sqhe->skhe', score_grad, query_heads, preferred_element_...  14.9 us
    dot_general x1, matrix products, body(): jnp.einsum('shqk,skhe->sqhe', score_grad, key_heads, preferred_element_ty...  14.1 us
  transfers between devices with their start and end apart: 8, of which 3 were waited for; matrix products, arithmetic and copies ran while one was open for 40% of the time, Pallas kernels for 0%

commit v1 on v0

--- a/solution.py
+++ b/solution.py
@@ -60,8 +60,14 @@
     row_count = steps_here * tokens_here
     action_count = actions.shape[1]
     score_scale = HD ** (-0.5)
-    full_both = lax.all_gather(
-        jnp.concatenate([hidden_in, out_grad], axis=0), "tensor", axis=3, tiled=True
+    full_both = jnp.concatenate(
+        lax.all_to_all(
+            jnp.stack([jnp.concatenate([hidden_in, out_grad], axis=0)] * lax.axis_size("tensor")),
+            "tensor",
+            0,
+            0,
+        ),
+        axis=3,
     )
     input_rows = full_both[0].reshape(row_count, model_width)
     grad_rows = full_both[1].reshape(row_count, model_width)

time: 511 us -> 604 us (1.18)
  waiting for transfers between devices: 211 us -> 259 us
  local copies, waits for them, and re-layouts: 149 us -> 192 us
    all_to_all x0 -> x1, waiting for transfers between devices: none -> 117 us  [body(): lax.all_to_all(jnp.stack([jnp.concatenate([hidden_in, out_grad], axis=0)]...]
    all_gather x1 -> x0, waiting for transfers between devices: 113 us -> none  [body(): lax.all_gather(jnp.concatenate([hidden_in, out_grad], axis=0), 'tensor',...]
    reduce_scatter x1, waiting for transfers between devices: 88.6 us -> 133 us  [body(): lax.psum_scatter(jnp.concatenate(pieces, axis=1), 'tm', scatter_dimension...]
    slice x1 -> x3, local copies, waits for them, and re-layouts: 8.73 us -> 29.4 us  [body(): grad_rows = full_both[1].reshape(row_count, model_width)]
    slice x0 -> x2, local copies, waits for them, and re-layouts: none -> 19.1 us  [body(): input_rows = full_both[0].reshape(row_count, model_width)]
    another operation x2 -> x1, local copies, waits for them, and re-layouts: 19.9 us -> 9.31 us  [body(): grad_split = grad_rows.reshape(row_count, tm_count, col_block)]
    dot_general x0 -> x1, local copies, waits for them, and re-layouts: none -> 8.85 us  [body(): jnp.dot(input_rows, branch_in, preferred_element_type=jnp.float32)]
    unnamed x84 -> x91, local copies, waits for them, and re-layouts: 68 us -> 70.4 us
  transfers between devices with their start and end apart: 8 -> 8, of which waited for: 3 -> 3; matrix products, arithmetic and copies ran while one was open for 40% -> 35% of each run, Pallas kernels for 0% -> 0%
where the time goes in v1:
time: 604 us; the launch traced here: 593 us
  waiting for transfers between devices  259 us (43%)
  local copies, waits for them, and re-layouts  192 us (32%)
  matrix products  96.5 us (16%)
  other arithmetic  15.3 us (3%)
  between operations  15.2 us (3%)
  starting transfers between devices  15 us (2%)
    reduce_scatter x1, waiting for transfers between devices, body(): lax.psum_scatter(jnp.concatenate(pieces, axis=1), 'tm', scatter_dimension...  133 us
    all_to_all x1, waiting for transfers between devices, body(): lax.all_to_all(jnp.stack([jnp.concatenate([hidden_in, out_grad], axis=0)]...  117 us
    unnamed x91, local copies, waits for them, and re-layouts  70.4 us
    slice x3, local copies, waits for them, and re-layouts, body(): grad_rows = full_both[1].reshape(row_count, model_width)  29.4 us
    concatenate x1, local copies, waits for them, and re-layouts, body(): jnp.concatenate(pieces, axis=1)  22.6 us
    dot_general x3, matrix products, contract_cols(): lax.dot_general(left, right, (((1,), (1,)), ((), ())), preferred_element_...  20 us
    slice x2, local copies, waits for them, and re-layouts, body(): input_rows = full_both[0].reshape(row_count, model_width)  19.1 us
    dot_general x1, matrix products, body(): jnp.einsum('shqk,sqhe->skhe', score_grad, query_heads, preferred_element_...  14.4 us
  transfers between devices with their start and end apart: 8, of which 3 were waited for; matrix products, arithmetic and copies ran while one was open for 35% of the time, Pallas kernels for 0%

profile of v1, /device:TPU:0, one launch (start us, length us, event | category | flops | bytes accessed | tf_op | source)
XLA Modules:
  0.0 593.3 jit_solution(7581171617489251390)
XLA Ops:
  8.8 5.3 stack.35
  14.1 5.9 all-to-all-start
  20.2 116.7 %all-to-all-done = bf16[8,2,2,256,640]{4,3,2,1,0:T(8,128)(2,1)} async-done(((bf16[8,2,2,256,640]{4,3,2,1,0:T(8,128)(2,1)}), bf16[8,2,2,256,640]{4,3,2,1,0:T(8,128)(2,1)}, u32[]{:S(2)}, u32[]{:S(2)}) %all-to-all-start) | async-done | bytes 10485792 | tf_op jit(solution)/shard_map/all_to_all | solution.py:64
  136.9 9.6 %fusion.76 = (bf16[1,2,256,8,640]{4,2,1,0,3:T(8,128)(2,1)}, bf16[1,2,256,8,640]{4,2,1,0,3:T(8,128)(2,1)}) fusion(bf16[2,2,256,8,640]{4,2,1,0,3:T(8,128)(2,1)} %bitcast.12), kind=kLoop, calls=%fused_computation.103 | loop fusion | bytes 20971520 | tf_op jit(solution)/shard_map/slice | solution.py:73
  146.5 5.7 copy.194
  152.2 3.6 copy.241
  155.8 5.4 copy.188
  161.1 8.9 %dot_general.56 = bf16[2,4,64,5120]{3,2,1,0:T(8,128)(2,1)} reshape(bf16[1,2,256,8,640]{4,3,2,1,0:T(8,128)(2,1)} %copy.188) | data formatting | bytes 10485760 | tf_op jit(solution)/shard_map/dot_general | solution.py:125
  170.0 6.5 %fusion.44 = (bf16[2,4,64,320]{3,2,1,0:T(8,128)(2,1)}, f32[2,4,64,320]{3,2,1,0:T(8,128)}) fusion(f32[4,320]{1,0:T(4,128)S(1)} %fusion.60, bf16[2,4,64,5120]{3,2,1,0:T(8,128)(2,1)} %dot_general.56, bf16[5120,320]{0,1:T(8,128)(2,1)S(1)} %copy-done), kind=kOutput, calls=%fused_computation.56 | convolution fusion | flops 1679360000 | bytes 9507840 | tf_op jit(solution)/shard_map/dot_general | solution.py:125
  176.5 2.2 copy.189
  178.7 5.7 fusion.39
  185.2 4.7 convolution_convert_fusion
  189.8 13.6 %copy.235 = bf16[1,2,256,5120]{2,1,0,3:T(2,128)(2,1)} copy(bf16[1,2,256,5120]{3,2,1,0:T(8,128)(2,1)} %bitcast.142) | data formatting | bytes 10485760
  203.4 5.7 copy.244
  211.3 2.5 collective-permute-start.1
  213.7 4.0 collective-permute-start
  220.6 1.8 fusion.78
  222.7 9.4 %collective-permute-done = bf16[2,256,640]{1,2,0:T(8,128)(2,1)} collective-permute-done((bf16[2,256,640]{1,2,0:T(8,128)(2,1)}, bf16[2,256,640]{1,2,0:T(8,128)(2,1)}, u32[]{:S(2)}, u32[]{:S(2)}) %collective-permute-start) | collective-permute-done | bytes 655392 | tf_op jit(solution)/shard_map/ppermute | solution.py:14
  237.5 2.6 fusion.79
  241.6 2.5 copy-done.28
  246.3 4.4 fusion.80
  250.8 4.8 add_convert_fusion
  255.6 13.7 %copy.233 = bf16[1,2,256,5120]{2,1,0,3:T(2,128)(2,1)} copy(bf16[1,2,256,5120]{3,2,1,0:T(8,128)(2,1)} %bitcast.136) | data formatting | bytes 10485760
  269.3 5.7 copy.243
  275.0 14.1 %copy.209 = bf16[1,2,256,8,640]{2,1,4,3,0:T(2,128)(2,1)} copy(bf16[1,2,256,8,640]{4,2,1,0,3:T(8,128)(2,1)} %get-tuple-element.64) | data formatting | bytes 10485760 | tf_op jit(solution)/shard_map/slice | solution.py:73
  289.2 13.7 %copy.211 = bf16[1,2,256,8,640]{2,1,4,3,0:T(2,128)(2,1)} copy(bf16[1,2,256,8,640]{4,2,1,0,3:T(8,128)(2,1)} %get-tuple-element.65) | data formatting | bytes 10485760 | tf_op jit(solution)/shard_map/slice | solution.py:72
  303.1 9.3 %reshape_reshape_squeeze.6 = bf16[512,16,320]{0,2,1:T(8,128)(2,1)} reshape(bf16[1,2,256,8,640]{2,1,4,3,0:T(2,128)(2,1)} %copy.209) | data formatting | bytes 10485760 | tf_op jit(solution)/shard_map/reshape;reshape;squeeze | solution.py:146
  312.4 9.2 %reshape_reshape_squeeze.7 = bf16[512,16,320]{0,2,1:T(8,128)(2,1)} reshape(bf16[1,2,256,8,640]{2,1,4,3,0:T(2,128)(2,1)} %copy.211) | data formatting | bytes 10485760 | tf_op jit(solution)/shard_map/reshape;reshape;squeeze | solution.py:149
  322.7 6.8 %convolution_convert_fusion.2 = bf16[16,320,320]{1,2,0:T(8,128)(2,1)} fusion(bf16[512,16,320]{0,2,1:T(8,128)(2,1)} %reshape_reshape_squeeze.7, bf16[512,320]{0,1:T(8,128)(2,1)} %copy-done.16), kind=kOutput, calls=%fused_computation.23 | convolution fusion | flops 1679360000 | bytes 8847360 | tf_op jit(solution)/shard_map/rjk,rn->jkn/dot_general | solution.py:147
  329.5 7.6 %convert_bitcast_fusion = bf16[16,320,320]{1,2,0:T(8,128)(2,1)} fusion(bf16[512,16,320]{0,2,1:T(8,128)(2,1)} %reshape_reshape_squeeze.6, bf16[512,320,1]{1,0,2:T(8,128)(2,1)S(1)} %bitcast.178), kind=kOutput, calls=%fused_computation.14 | convolution fusion | flops 1679360000 | bytes 8847360 | tf_op jit(solution)/shard_map/rk,rjn->jkn/dot_general | solution.py:153
  337.0 6.3 %fusion.7 = bf16[16,640,320]{1,2,0:T(8,128)(2,1)} fusion(bf16[512,16,320]{0,2,1:T(8,128)(2,1)S(1)} %bitcast.148, bf16[512,640]{0,1:T(8,128)(2,1)S(1)} %bitcast.159), kind=kOutput, calls=%fused_computation.13 | convolution fusion | flops 3358720000 | bytes 12451840 | tf_op jit(solution)/shard_map/rk,rjn->jkn/dot_general | solution.py:161
  343.3 22.6 %concatenate.27 = bf16[16,1288,320]{1,2,0:T(8,128)(2,1)} concatenate(bf16[16,640,320]{1,2,0:T(8,128)(2,1)} %fusion.7, bf16[16,320,320]{1,2,0:T(8,128)(2,1)} %convolution_convert_fusion.2, bf16[16,320,320]{1,2,0:T(8,128)(2,1)} %convert_bitcast_fusion, bf16[16,8,320]{1,2,0:T(8,128)(2,1)S(1)} %copy.214), dimensions={1} | concatenate | bytes 26378240 | tf_op jit(solution)/shard_map/concatenate | solution.py:170
  365.9 9.6 %convolution_convert_fusion.3 = bf16[512,640]{1,0:T(8,128)(2,1)} fusion(bf16[512,5120]{1,0:T(8,128)(2,1)} %bitcast.146, bf16[640,5120]{1,0:T(8,128)(2,1)} %param.17), kind=kOutput, calls=%fused_computation.34 | convolution fusion | flops 3355770880 | bytes 12451840 | tf_op jit(solution)/shard_map/dot_general | solution.py:36
  375.5 2.0 reshape.151
  378.8 5.1 fusion.21
  383.9 2.0 copy-done.4
  387.0 4.4 fusion.26
  391.4 14.4 %fusion.11 = f32[2,5,768,128]{2,3,1,0:T(8,128)} fusion(bf16[2,256,5,128]{1,3,2,0:T(8,128)(2,1)S(1)} %bitcast.155, f32[2,5,256,768]{2,3,1,0:T(8,128)} %fusion.26, f32[2,5,256,768]{2,3,1,0:T(8,128)} %copy-done.28, f32[2,5,256]{2,1,0:T(8,128)S(1)} %get-tuple-element.72), kind=kOutput, calls=%fused_computation.15 | convolution fusion | flops 517082368 | bytes 20326400 | tf_op jit(solution)/shard_map/shqk,sqhe->skhe/dot_general | solution.py:199
  405.9 2.1 slice_reduce_fusion.3
  416.2 13.2 %fusion.30 = bf16[2,5,128,256]{3,2,1,0:T(8,128)(2,1)S(1)} fusion(f32[2,5,256,768]{2,3,1,0:T(8,128)} %fusion.26, bf16[2,256,5,128]{3,1,2,0:T(8,128)(2,1)S(1)} %copy.183, bf16[2,256,5,128]{3,1,2,0:T(8,128)(2,1)S(1)} %copy-done.9, bf16[2,256,5,128]{3,1,2,0:T(8,128)(2,1)S(1)} %copy-done.11, f32[2,5,256,768]{2,3,1,0:T(8,128)} %copy-done.28, ...), kind=kOutput, calls=%fused_computation.33 | convolution fusion | flops 523308288 | bytes 18360320 | tf_op jit(solution)/shard_map/shqk,skhe->sqhe/dot_general | solution.py:195
  434.5 2.0 reshape.150
  436.5 1.9 copy.236
  438.5 2.0 reshape.148
  440.5 1.9 copy.234
  442.5 3.4 add_convert_fusion.1
  445.8 132.6 %reduce-scatter.8.cloned.1.call-done = bf16[1,1288,320]{1,2,0:T(8,128)(2,1)} async-done(((bf16[16,1288,320]{1,2,0:T(8,128)(2,1)}), bf16[1,1288,320]{1,2,0:T(8,128)(2,1)}) %reduce-scatter.8.cloned.1.call-update) | async-done | bytes 824336 | tf_op jit(solution)/shard_map/reduce_scatter | solution.py:169
  582.5 2.0 copy.218
  584.5 2.0 copy.217
  (127 shorter events, 37.0 us)
Async XLA Ops:
  7.2 162.8 %copy-start = (bf16[5120,320]{0,1:T(8,128)(2,1)S(1)}, bf16[5120,320]{0,1:T(8,128)(2,1)}, u32[]{:S(2)}) copy-start(bf16[5120,320]{0,1:T(8,128)(2,1)} %param.18) | copy-start | bytes 9830404
  14.1 5.9 %copy-start.25 = (s32[1,4]{1,0:T(1,128)S(1)}, s32[1,4]{1,0:T(1,128)}, u32[]{:S(2)}) copy-start(s32[1,4]{1,0:T(1,128)} %param.21) | copy-start | bytes 52
  14.1 6.0 %copy-start.26 = (bf16[128,320]{0,1:T(8,128)(2,1)S(1)}, bf16[128,320]{0,1:T(8,128)(2,1)}, u32[]{:S(2)}) copy-start(bf16[128,320]{0,1:T(8,128)(2,1)} %param.20) | copy-start | bytes 245764
  14.1 122.8 %all-to-all-start = ((bf16[8,2,2,256,640]{4,3,2,1,0:T(8,128)(2,1)}), bf16[8,2,2,256,640]{4,3,2,1,0:T(8,128)(2,1)}, u32[]{:S(2)}, u32[]{:S(2)}) async-start(bf16[8,2,2,256,640]{4,3,2,1,0:T(8,128)(2,1)} %stack.35), calls=%async_computation | async-start | bytes 20971520 | tf_op jit(solution)/shard_map/all_to_all | solution.py:64
  20.0 414.5 %reduce-scatter.12.cloned.1.call-start = ((), (), s32[]{:S(2)}) async-start(), calls=%async_computation.6 | async-start | bytes 5898240
  146.5 9.2 %slice-start = ((s8[5242880]{0:T(1024)(128)(4,1)}), s8[4194304]{0:T(1024)(128)(4,1)S(1)}, s32[]{:S(2)}) async-start(s8[5242880]{0:T(1024)(128)(4,1)} %bitcast.134), calls=%async_computation.7 | async-start | bytes 8388608
  152.2 3.6 slice-start.1
  184.4 0.7 copy-start.16
  209.1 1.1 copy-start.22
  209.1 9.3 %copy-start.23 = (bf16[1,2,256,640]{3,2,1,0:T(8,128)(2,1)S(1)}, bf16[1,2,256,640]{3,2,1,0:T(8,128)(2,1)}, u32[]{:S(2)}) copy-start(bf16[1,2,256,640]{3,2,1,0:T(8,128)(2,1)} %param.13) | copy-start | bytes 1966084
  209.1 9.5 %copy-start.24 = (bf16[1,2,256,640]{3,2,1,0:T(8,128)(2,1)S(1)}, bf16[1,2,256,640]{3,2,1,0:T(8,128)(2,1)}, u32[]{:S(2)}) copy-start(bf16[1,2,256,640]{3,2,1,0:T(8,128)(2,1)} %param.14) | copy-start | bytes 1966084
  209.1 229.4 %reduce-scatter.10.cloned.1.call-start = ((), (), s32[]{:S(2)}) async-start(), calls=%async_computation.5 | async-start | bytes 5898240
  211.3 9.3 %collective-permute-start.1 = (bf16[2,256,640]{1,2,0:T(8,128)(2,1)}, bf16[2,256,640]{1,2,0:T(8,128)(2,1)}, u32[]{:S(2)}, u32[]{:S(2)}) collective-permute-start(bf16[2,256,640]{1,2,0:T(8,128)(2,1)} %bitcast), channel_id=1, source_target_pairs={{0,8},{8,16},{16,24},{24,32},{32,40},{40,48},{48,56},{56,64},{64,7... | collective-permute-start | bytes 1966088 | tf_op jit(solution)/shard_map/ppermute | solution.py:14
  213.7 18.4 %collective-permute-start = (bf16[2,256,640]{1,2,0:T(8,128)(2,1)}, bf16[2,256,640]{1,2,0:T(8,128)(2,1)}, u32[]{:S(2)}, u32[]{:S(2)}) collective-permute-start(bf16[2,256,640]{1,2,0:T(8,128)(2,1)} %bitcast), channel_id=1, source_target_pairs={{0,16},{8,24},{16,32},{24,40},{32,48},{40,56},{48,64},{56,72},{64,... | collective-permute-start | bytes 1966088 | tf_op jit(solution)/shard_map/ppermute | solution.py:14
  234.9 2.5 copy-start.8
  236.3 1.2 copy-start.10
  237.5 2.7 copy-start.20
  237.5 2.7 copy-start.21
  240.1 3.9 copy-start.28
  240.2 4.2 copy-start.12
  240.3 4.4 copy-start.14
  240.3 5.3 slice-start.2
  240.3 6.0 %slice-start.3 = ((s8[6553600]{0:T(1024)(128)(4,1)}), s8[2359296]{0:T(1024)(128)(4,1)S(1)}, s32[]{:S(2)}) async-start(s8[6553600]{0:T(1024)(128)(4,1)} %bitcast.143), calls=%async_computation.10 | async-start | bytes 4718592
  245.5 5.3 copy-start.5
  246.3 4.4 copy-start.2
  246.3 4.4 copy-start.3
  275.0 303.5 %reduce-scatter.8.cloned.1.call-start = ((), (), s32[]{:S(2)}) async-start(), calls=%async_computation.4 | async-start | bytes 15319040 | tf_op jit(solution)/shard_map/reduce_scatter | solution.py:169
  289.2 13.7 %copy-start.17 = (bf16[512,320]{0,1:T(8,128)(2,1)S(1)}, bf16[512,320]{0,1:T(8,128)(2,1)}, u32[]{:S(2)}) copy-start(bf16[512,320]{0,1:T(8,128)(2,1)} %copy-done.16) | copy-start | bytes 983044
  322.6 6.8 %copy-start.27 = (bf16[2,4,64,320]{3,2,1,0:T(8,128)(2,1)S(1)}, bf16[2,4,64,320]{3,2,1,0:T(8,128)(2,1)}, u32[]{:S(2)}) copy-start(bf16[2,4,64,320]{3,2,1,0:T(8,128)(2,1)} %get-tuple-element.74) | copy-start | bytes 983044
  322.6 14.4 %slice-start.4 = ((s8[5242880]{0:T(1024)(128)(4,1)}), s8[4194304]{0:T(1024)(128)(4,1)S(1)}, s32[]{:S(2)}) async-start(s8[5242880]{0:T(1024)(128)(4,1)} %bitcast.147), calls=%async_computation.11 | async-start | bytes 8388608
  329.5 7.6 %slice-start.5 = ((s8[5242880]{0:T(1024)(128)(4,1)}), s8[1048576]{0:T(1024)(128)(4,1)S(1)}, s32[]{:S(2)}) async-start(s8[5242880]{0:T(1024)(128)(4,1)} %bitcast.147), calls=%async_computation.12 | async-start | bytes 2097152
  329.5 7.6 %copy-start.6 = (bf16[80,8,2,256]{3,1,2,0:T(8,128)(2,1)S(1)}, bf16[80,8,2,256]{3,1,2,0:T(8,128)(2,1)}, u32[]{:S(2)}) copy-start(bf16[80,8,2,256]{3,1,2,0:T(8,128)(2,1)} %copy-done.5) | copy-start | bytes 1966084
  378.8 8.2 %copy-start.7 = (bf16[2,256,5,128]{1,3,2,0:T(8,128)(2,1)S(1)}, bf16[2,256,5,128]{1,3,2,0:T(8,128)(2,1)}, u32[]{:S(2)}) copy-start(bf16[2,256,5,128]{1,3,2,0:T(8,128)(2,1)} %copy.206) | copy-start | bytes 1966084
  378.8 8.2 %copy-start.13 = (bf16[2,256,5,128]{1,3,2,0:T(8,128)(2,1)S(1)}, bf16[2,256,5,128]{1,3,2,0:T(8,128)(2,1)}, u32[]{:S(2)}) copy-start(bf16[2,256,5,128]{1,3,2,0:T(8,128)(2,1)} %copy-done.12) | copy-start | bytes 1966084
  378.8 8.2 %copy-start.15 = (bf16[2,256,5,128]{1,3,2,0:T(8,128)(2,1)S(1)}, bf16[2,256,5,128]{1,3,2,0:T(8,128)(2,1)}, u32[]{:S(2)}) copy-start(bf16[2,256,5,128]{1,3,2,0:T(8,128)(2,1)} %copy-done.14) | copy-start | bytes 1966084
  383.9 2.0 copy-start.4
  391.4 16.5 %copy-start.19 = (bf16[256,640]{0,1:T(8,128)(2,1)S(1)}, bf16[256,640]{0,1:T(8,128)(2,1)}, u32[]{:S(2)}) copy-start(bf16[256,640]{0,1:T(8,128)(2,1)} %get-tuple-element.63) | copy-start | bytes 983044
  391.4 18.7 %copy-start.18 = (bf16[256,640]{0,1:T(8,128)(2,1)S(1)}, bf16[256,640]{0,1:T(8,128)(2,1)}, u32[]{:S(2)}) copy-start(bf16[256,640]{0,1:T(8,128)(2,1)} %get-tuple-element.62) | copy-start | bytes 983044
  405.9 10.3 %copy-start.9 = (bf16[2,256,5,128]{3,1,2,0:T(8,128)(2,1)S(1)}, bf16[2,256,5,128]{3,1,2,0:T(8,128)(2,1)}, u32[]{:S(2)}) copy-start(bf16[2,256,5,128]{3,1,2,0:T(8,128)(2,1)} %copy-done.8) | copy-start | bytes 1966084
  405.9 10.3 %copy-start.11 = (bf16[2,256,5,128]{3,1,2,0:T(8,128)(2,1)S(1)}, bf16[2,256,5,128]{3,1,2,0:T(8,128)(2,1)}, u32[]{:S(2)}) copy-start(bf16[2,256,5,128]{3,1,2,0:T(8,128)(2,1)} %copy-done.10) | copy-start | bytes 1966084
  408.9 22.7 %collective-permute-start.3 = (bf16[2,256,640]{1,2,0:T(8,128)(2,1)}, bf16[2,256,640]{1,2,0:T(8,128)(2,1)}, u32[]{:S(2)}, u32[]{:S(2)}) collective-permute-start(bf16[2,256,640]{1,2,0:T(8,128)(2,1)} %pad_maximum_fusion.14), channel_id=1, source_target_pairs={{16,0},{24,8},{32,16},{40,24},{48,32},{56,40},{64,48},{72,56},{80,... | collective-permute-start | bytes 1966088 | tf_op jit(solution)/shard_map/ppermute | solution.py:14
  411.1 20.6 %collective-permute-start.2 = (bf16[2,256,640]{1,2,0:T(8,128)(2,1)}, bf16[2,256,640]{1,2,0:T(8,128)(2,1)}, u32[]{:S(2)}, u32[]{:S(2)}) collective-permute-start(bf16[2,256,640]{1,2,0:T(8,128)(2,1)} %pad_maximum_fusion.13), channel_id=1, source_target_pairs={{8,0},{16,8},{24,16},{32,24},{40,32},{48,40},{56,48},{64,56},{72,6... | collective-permute-start | bytes 1966088 | tf_op jit(solution)/shard_map/ppermute | solution.py:14
  442.5 144.1 %copy-start.1 = (bf16[5120,320]{0,1:T(8,128)(2,1)S(1)}, bf16[5120,320]{0,1:T(8,128)(2,1)}, u32[]{:S(2)}) copy-start(bf16[5120,320]{0,1:T(8,128)(2,1)} %param.18) | copy-start | bytes 9830404
Sparse Core Ops, SparseCore 0:
  209.2 121.2 reduce-scatter.11
  333.0 72.7 reduce-scatter.9
  410.3 168.1 reduce-scatter.7
